TPU v7x, 32 devices: a whole 2x2x4 slice. The times are simulated.
32 devices in a mesh: fsdp: 8 (over z, y), dp: 4 (over x, core).
Axes of the slice: x: 2, y: 2, z: 4, core: 2. Of those that a mesh axis runs over, the one named last changes fastest.
Arguments:
- tokens: bfloat16 [32768, 768], P(('fsdp', 'dp')), may hold values from -6 to 6
- image_table: int32 [160, 3], P(('fsdp', 'dp')), may hold values from 0 to 996, as said below
- ln1_gain: bfloat16 [768], P('fsdp'), may hold values from 0.5 to 1.5
- ln1_bias: bfloat16 [768], P('fsdp'), may hold values from -3 to 3
- qkv_weight: bfloat16 [768, 2304], P('fsdp'), may hold values from -0.21875 to 0.21875
- qkv_bias: bfloat16 [2304], P('fsdp'), may hold values from -2 to 2
- out_weight: bfloat16 [768, 768], P('fsdp'), may hold values from -0.875 to 0.875
- out_bias: bfloat16 [768], P('fsdp'), may hold values from -2 to 2
- ln2_gain: bfloat16 [768], P('fsdp'), may hold values from 0.5 to 1.5
- ln2_bias: bfloat16 [768], P('fsdp'), may hold values from -3 to 3
- fc1_weight: bfloat16 [768, 3072], P('fsdp'), may hold values from -0.21875 to 0.21875
- fc1_bias: bfloat16 [3072], P('fsdp'), may hold values from -3 to 3
- fc2_weight: bfloat16 [3072, 768], P('fsdp'), may hold values from -0.109375 to 0.109375
- fc2_bias: bfloat16 [768], P('fsdp'), may hold values from -2 to 2
- frequencies: bfloat16 [768], P('fsdp'), may hold values from -0.796875 to 0.796875
- cotangent: bfloat16 [32768, 768], P(('fsdp', 'dp')), may hold values from -6 to 6
Outputs:
- block_out: bfloat16 [32768, 768], P(('fsdp', 'dp'))
- tokens_grad: bfloat16 [32768, 768], P(('fsdp', 'dp'))
- first_norm_gain_gradient: float32 [768], P('fsdp')
- ln1_bias_grad: float32 [768], P('fsdp')
- qkv_weight_grad: float32 [768, 2304], P('fsdp')
- qkv_bias_grad: float32 [2304], P('fsdp')
- out_weight_grad: float32 [768, 768], P('fsdp')
- out_bias_grad: float32 [768], P('fsdp')
- second_norm_gain_gradient: float32 [768], P('fsdp')
- ln2_bias_grad: float32 [768], P('fsdp')
- fc1_weight_grad: float32 [768, 3072], P('fsdp')
- fc1_bias_grad: float32 [3072], P('fsdp')
- fc2_weight_grad: float32 [3072, 768], P('fsdp')
- fc2_bias_grad: float32 [768], P('fsdp')
- frequencies_grad: float32 [768], P('fsdp')
- freq_grad_norm: float32 [], replicated
- other_grad_norm: float32 [], replicated
Inputs may be any that keep to these rules, and one draw needn't show every extreme that they name: `image_table`: rows 5b to 5b+4 describe bin b: either a 24x24 and a 20x20 image, or 24x24 and two 14x14, or two 20x20 and one 14x14, or one 20x20 and three 14x14, or five 14x14, laid end to end from offset 0 in the listed order; unused rows have height and width 0 and the offset where the used rows end. Grids are square.
All inputs are finite; a program needn't handle non-finite values.
Results may differ from a plain program's by a relative error of at most 0.015.
Values may be sent and summed in bfloat16 or wider, within the bound.
No kernel may reach another device: no remote copies, remote signals or barrier semaphores. Data moves between devices by JAX's collectives and lax.ppermute only.
A program may use at most 192 MiB of HBM per device.

v0:
```python
import jax
import jax.numpy as jnp
from jax import lax
from jax.sharding import PartitionSpec as P

H = 12
HD = 64
BIN = 1024
norm_eps = 1e-06
masked_score = -1e30
inv_sqrt_two_pi = 0.3989422804014327


def matmul(left, right):
    return jnp.dot(left, right, preferred_element_type=jnp.float32)


def matmul_left_t(left, right):
    return lax.dot_general(
        left, right, (((0,), (0,)), ((), ())), preferred_element_type=jnp.float32
    )


def matmul_right_t(left, right):
    return lax.dot_general(
        left, right, (((1,), (1,)), ((), ())), preferred_element_type=jnp.float32
    )


def image_layout(image_table, bin_count, bin_rows):
    slot_count = image_table.shape[0] // bin_count
    table = image_table.reshape(bin_count, slot_count, 3)
    offset = table[:, :, 0:1]
    height = table[:, :, 1:2]
    width = table[:, :, 2:3]
    place = jnp.arange(bin_rows, dtype=jnp.int32)[None, None, :]
    inside = ((place >= offset) & (place < offset + height * width)).astype(jnp.int32)
    live = jnp.sum(inside, axis=1)
    slot_ids = jnp.arange(slot_count, dtype=jnp.int32)[None, :, None]
    segment = jnp.sum(inside * slot_ids, axis=1) + slot_count * (1 - live)
    local_place = place[:, 0, :] - jnp.sum(inside * offset, axis=1)
    grid_width = jnp.maximum(jnp.sum(inside * width, axis=1), 1)
    grid_row = local_place // grid_width * live
    grid_col = local_place % grid_width * live
    return (
        segment,
        grid_row.reshape(-1).astype(jnp.float32),
        grid_col.reshape(-1).astype(jnp.float32),
    )


def rotary_tables(frequencies, grid_row, grid_col):
    half_width = frequencies.shape[0] // 2
    freq_float = frequencies.astype(jnp.float32)
    freq_row = freq_float[:half_width].reshape(H, HD // 2)
    freq_col = freq_float[half_width:].reshape(H, HD // 2)
    theta = grid_row[:, None, None] * freq_row[None] + grid_col[:, None, None] * freq_col[None]
    return (jnp.cos(theta), jnp.sin(theta))


def rotate(heads, cosine, sine):
    half_width = heads.shape[-1] // 2
    first = heads[..., :half_width]
    second = heads[..., half_width:]
    return jnp.concatenate(
        [first * cosine - second * sine, first * sine + second * cosine], axis=-1
    )


def layer_norm_forward(values):
    center = values - jnp.mean(values, axis=-1, keepdims=True)
    inverse_deviation = lax.rsqrt(jnp.mean(center * center, axis=-1, keepdims=True) + norm_eps)
    return (center * inverse_deviation, inverse_deviation)


def layer_norm_backward(
    gradient_norm_total, centered_normalized, inverse_deviation, norm_gain_vector
):
    gain_scaled_output = gradient_norm_total * norm_gain_vector
    return inverse_deviation * (
        gain_scaled_output
        - jnp.mean(gain_scaled_output, axis=-1, keepdims=True)
        - centered_normalized
        * jnp.mean(gain_scaled_output * centered_normalized, axis=-1, keepdims=True)
    )


def gelu_slope(values):
    return (
        0.5 * (1.0 + lax.erf(values * 0.7071067811865476))
        + values * jnp.exp(-0.5 * values * values) * inv_sqrt_two_pi
    )


def join_heads(stacked):
    return jnp.transpose(stacked, (1, 0, 2)).reshape(stacked.shape[1], H * HD)


def head_slice(matrix, head_index):
    return lax.dynamic_slice_in_dim(matrix, head_index * HD, HD, 1)


def attend_bin(packed):
    query, key_rows, value, segment = packed
    mask = segment[:, None] == segment[None, :]
    scale = HD ** (-0.5)

    def one_head(head_index):
        q_head = head_slice(query, head_index)
        k_head = head_slice(key_rows, head_index)
        v_head = head_slice(value, head_index)
        scores = jnp.where(mask, matmul_right_t(q_head, k_head) * scale, masked_score)
        top = jnp.max(scores, axis=-1, keepdims=True)
        log_total = top + jnp.log(jnp.sum(jnp.exp(scores - top), axis=-1, keepdims=True))
        probs = jnp.exp(scores - log_total).astype(jnp.bfloat16)
        return (matmul(probs, v_head).astype(jnp.bfloat16), log_total[:, 0])

    mixed, log_total = lax.map(one_head, jnp.arange(H, dtype=jnp.int32))
    return (join_heads(mixed), log_total)


def attend_bin_back(packed):
    query, key_rows, value, d_mixed, log_total, segment = packed
    mask = segment[:, None] == segment[None, :]
    scale = HD ** (-0.5)

    def one_head(head_index):
        q_head = head_slice(query, head_index)
        k_head = head_slice(key_rows, head_index)
        v_head = head_slice(value, head_index)
        d_head = head_slice(d_mixed, head_index)
        total_head = lax.dynamic_index_in_dim(log_total, head_index, 0, keepdims=False)
        scores = jnp.where(mask, matmul_right_t(q_head, k_head) * scale, masked_score)
        probs = jnp.exp(scores - total_head[:, None])
        d_probs = matmul_right_t(d_head, v_head)
        d_value = matmul_left_t(probs.astype(jnp.bfloat16), d_head)
        inner = jnp.sum(probs * d_probs, axis=-1, keepdims=True)
        d_scores = (probs * (d_probs - inner)).astype(jnp.bfloat16)
        d_query = matmul(d_scores, k_head) * scale
        d_key = matmul_left_t(d_scores, q_head) * scale
        return (d_query, d_key, d_value)

    d_query, d_key, d_value = lax.map(one_head, jnp.arange(H, dtype=jnp.int32))
    return (join_heads(d_query), join_heads(d_key), join_heads(d_value))


def square_sums(pieces):
    freq_sq = jnp.sum(pieces[12] * pieces[12])
    other_sq = jnp.float32(0.0)
    for member in pieces[:12]:
        other_sq = other_sq + jnp.sum(member * member)
    return (freq_sq, other_sq)


def shards(
    tokens,
    image_table,
    ln1_gain,
    ln1_bias,
    qkv_weight,
    qkv_bias,
    out_weight,
    out_bias,
    ln2_gain,
    ln2_bias,
    fc1_weight,
    fc1_bias,
    fc2_weight,
    fc2_bias,
    frequencies,
    cotangent,
):
    block_parameters = (
        lax.all_gather(ln1_gain, "fsdp", axis=0, tiled=True),
        lax.all_gather(ln1_bias, "fsdp", axis=0, tiled=True),
        lax.all_gather(qkv_weight, "fsdp", axis=0, tiled=True),
        lax.all_gather(qkv_bias, "fsdp", axis=0, tiled=True),
        lax.all_gather(out_weight, "fsdp", axis=0, tiled=True),
        lax.all_gather(out_bias, "fsdp", axis=0, tiled=True),
        lax.all_gather(ln2_gain, "fsdp", axis=0, tiled=True),
        lax.all_gather(ln2_bias, "fsdp", axis=0, tiled=True),
        lax.all_gather(fc1_weight, "fsdp", axis=0, tiled=True),
        lax.all_gather(fc1_bias, "fsdp", axis=0, tiled=True),
        lax.all_gather(fc2_weight, "fsdp", axis=0, tiled=True),
        lax.all_gather(fc2_bias, "fsdp", axis=0, tiled=True),
        lax.all_gather(frequencies, "fsdp", axis=0, tiled=True),
    )
    row_count, width = tokens.shape
    bin_count = row_count // BIN
    half_head = HD // 2
    segment, grid_row, grid_col = image_layout(image_table, bin_count, BIN)
    cosine, sine = rotary_tables(block_parameters[12], grid_row, grid_col)
    input_single_precision = tokens.astype(jnp.float32)
    first_centered_normalized, first_inverse_deviation = layer_norm_forward(input_single_precision)
    first_activation = (
        first_centered_normalized * block_parameters[0].astype(jnp.float32)
        + block_parameters[1].astype(jnp.float32)
    ).astype(jnp.bfloat16)
    qkv_full = matmul(first_activation, block_parameters[2]) + block_parameters[3].astype(
        jnp.float32
    )
    q_rot = rotate(qkv_full[:, :width].reshape(row_count, H, HD), cosine, sine)
    k_rot = rotate(qkv_full[:, width : 2 * width].reshape(row_count, H, HD), cosine, sine)
    q_low = q_rot.reshape(row_count, width).astype(jnp.bfloat16)
    k_low = k_rot.reshape(row_count, width).astype(jnp.bfloat16)
    v_low = qkv_full[:, 2 * width :].astype(jnp.bfloat16)
    q_bins = q_low.reshape(bin_count, BIN, width)
    k_bins = k_low.reshape(bin_count, BIN, width)
    v_bins = v_low.reshape(bin_count, BIN, width)
    mixed, log_total = lax.map(attend_bin, (q_bins, k_bins, v_bins, segment))
    mixed = mixed.reshape(row_count, width)
    residual_stream = (
        input_single_precision
        + matmul(mixed, block_parameters[4])
        + block_parameters[5].astype(jnp.float32)
    )
    second_centered_normalized, second_inverse_deviation = layer_norm_forward(residual_stream)
    second_activation = (
        second_centered_normalized * block_parameters[6].astype(jnp.float32)
        + block_parameters[7].astype(jnp.float32)
    ).astype(jnp.bfloat16)
    up_proj = matmul(second_activation, block_parameters[8]) + block_parameters[9].astype(
        jnp.float32
    )
    gelu_low = jax.nn.gelu(up_proj, approximate=False).astype(jnp.bfloat16)
    block_out = (
        residual_stream
        + matmul(gelu_low, block_parameters[10])
        + block_parameters[11].astype(jnp.float32)
    ).astype(jnp.bfloat16)
    block_parameters = (
        lax.all_gather(ln1_gain, "fsdp", axis=0, tiled=True),
        lax.all_gather(ln1_bias, "fsdp", axis=0, tiled=True),
        lax.all_gather(qkv_weight, "fsdp", axis=0, tiled=True),
        lax.all_gather(qkv_bias, "fsdp", axis=0, tiled=True),
        lax.all_gather(out_weight, "fsdp", axis=0, tiled=True),
        lax.all_gather(out_bias, "fsdp", axis=0, tiled=True),
        lax.all_gather(ln2_gain, "fsdp", axis=0, tiled=True),
        lax.all_gather(ln2_bias, "fsdp", axis=0, tiled=True),
        lax.all_gather(fc1_weight, "fsdp", axis=0, tiled=True),
        lax.all_gather(fc1_bias, "fsdp", axis=0, tiled=True),
        lax.all_gather(fc2_weight, "fsdp", axis=0, tiled=True),
        lax.all_gather(fc2_bias, "fsdp", axis=0, tiled=True),
        lax.all_gather(frequencies, "fsdp", axis=0, tiled=True),
    )
    output_gradient = cotangent.astype(jnp.float32)
    fc2_bias_grad = jnp.sum(output_gradient, axis=0)
    fc2_weight_grad = matmul_left_t(gelu_low, cotangent)
    d_up = (matmul_right_t(cotangent, block_parameters[10]) * gelu_slope(up_proj)).astype(
        jnp.bfloat16
    )
    fc1_bias_grad = jnp.sum(d_up.astype(jnp.float32), axis=0)
    fc1_weight_grad = matmul_left_t(second_activation, d_up)
    second_activation_gradient = matmul_right_t(d_up, block_parameters[8])
    second_norm_gain_gradient = jnp.sum(
        second_activation_gradient * second_centered_normalized, axis=0
    )
    ln2_bias_grad = jnp.sum(second_activation_gradient, axis=0)
    residual_gradient = output_gradient + layer_norm_backward(
        second_activation_gradient,
        second_centered_normalized,
        second_inverse_deviation,
        block_parameters[6].astype(jnp.float32),
    )
    d_att = residual_gradient.astype(jnp.bfloat16)
    out_bias_grad = jnp.sum(d_att.astype(jnp.float32), axis=0)
    out_weight_grad = matmul_left_t(mixed, d_att)
    d_mixed = matmul_right_t(d_att, block_parameters[4]).astype(jnp.bfloat16)
    d_qrot, d_krot, d_value = lax.map(
        attend_bin_back,
        (q_bins, k_bins, v_bins, d_mixed.reshape(bin_count, BIN, width), log_total, segment),
    )
    d_qrot = d_qrot.reshape(row_count, H, HD)
    d_krot = d_krot.reshape(row_count, H, HD)
    d_theta = (
        d_qrot[..., half_head:] * q_rot[..., :half_head]
        - d_qrot[..., :half_head] * q_rot[..., half_head:]
    )
    d_theta = (
        d_theta
        + d_krot[..., half_head:] * k_rot[..., :half_head]
        - d_krot[..., :half_head] * k_rot[..., half_head:]
    )
    frequencies_grad = jnp.concatenate(
        [
            jnp.sum(grid_row[:, None, None] * d_theta, axis=0).reshape(-1),
            jnp.sum(grid_col[:, None, None] * d_theta, axis=0).reshape(-1),
        ]
    )
    d_query = rotate(d_qrot, cosine, -sine).reshape(row_count, width)
    d_key = rotate(d_krot, cosine, -sine).reshape(row_count, width)
    d_qkv = jnp.concatenate([d_query, d_key, d_value.reshape(row_count, width)], axis=1).astype(
        jnp.bfloat16
    )
    qkv_bias_grad = jnp.sum(d_qkv.astype(jnp.float32), axis=0)
    qkv_weight_grad = matmul_left_t(first_activation, d_qkv)
    first_activation_gradient = matmul_right_t(d_qkv, block_parameters[2])
    first_norm_gain_gradient = jnp.sum(
        first_activation_gradient * first_centered_normalized, axis=0
    )
    ln1_bias_grad = jnp.sum(first_activation_gradient, axis=0)
    tokens_grad = (
        residual_gradient
        + layer_norm_backward(
            first_activation_gradient,
            first_centered_normalized,
            first_inverse_deviation,
            block_parameters[0].astype(jnp.float32),
        )
    ).astype(jnp.bfloat16)
    pieces = (
        lax.psum_scatter(first_norm_gain_gradient, "fsdp", scatter_dimension=0, tiled=True),
        lax.psum_scatter(ln1_bias_grad, "fsdp", scatter_dimension=0, tiled=True),
        lax.psum_scatter(qkv_weight_grad, "fsdp", scatter_dimension=0, tiled=True),
        lax.psum_scatter(qkv_bias_grad, "fsdp", scatter_dimension=0, tiled=True),
        lax.psum_scatter(out_weight_grad, "fsdp", scatter_dimension=0, tiled=True),
        lax.psum_scatter(out_bias_grad, "fsdp", scatter_dimension=0, tiled=True),
        lax.psum_scatter(second_norm_gain_gradient, "fsdp", scatter_dimension=0, tiled=True),
        lax.psum_scatter(ln2_bias_grad, "fsdp", scatter_dimension=0, tiled=True),
        lax.psum_scatter(fc1_weight_grad, "fsdp", scatter_dimension=0, tiled=True),
        lax.psum_scatter(fc1_bias_grad, "fsdp", scatter_dimension=0, tiled=True),
        lax.psum_scatter(fc2_weight_grad, "fsdp", scatter_dimension=0, tiled=True),
        lax.psum_scatter(fc2_bias_grad, "fsdp", scatter_dimension=0, tiled=True),
        lax.psum_scatter(frequencies_grad, "fsdp", scatter_dimension=0, tiled=True),
    )
    pieces = (
        lax.psum(pieces[0].astype(jnp.bfloat16), "dp").astype(jnp.float32),
        lax.psum(pieces[1].astype(jnp.bfloat16), "dp").astype(jnp.float32),
        lax.psum(pieces[2].astype(jnp.bfloat16), "dp").astype(jnp.float32),
        lax.psum(pieces[3].astype(jnp.bfloat16), "dp").astype(jnp.float32),
        lax.psum(pieces[4].astype(jnp.bfloat16), "dp").astype(jnp.float32),
        lax.psum(pieces[5].astype(jnp.bfloat16), "dp").astype(jnp.float32),
        lax.psum(pieces[6].astype(jnp.bfloat16), "dp").astype(jnp.float32),
        lax.psum(pieces[7].astype(jnp.bfloat16), "dp").astype(jnp.float32),
        lax.psum(pieces[8].astype(jnp.bfloat16), "dp").astype(jnp.float32),
        lax.psum(pieces[9].astype(jnp.bfloat16), "dp").astype(jnp.float32),
        lax.psum(pieces[10].astype(jnp.bfloat16), "dp").astype(jnp.float32),
        lax.psum(pieces[11].astype(jnp.bfloat16), "dp").astype(jnp.float32),
        lax.psum(pieces[12].astype(jnp.bfloat16), "dp").astype(jnp.float32),
    )
    freq_sq, other_sq = square_sums(pieces)
    freq_sq, other_sq = lax.psum((freq_sq, other_sq), "fsdp")
    return (
        block_out,
        tokens_grad,
        pieces[0],
        pieces[1],
        pieces[2],
        pieces[3],
        pieces[4],
        pieces[5],
        pieces[6],
        pieces[7],
        pieces[8],
        pieces[9],
        pieces[10],
        pieces[11],
        pieces[12],
        jnp.sqrt(freq_sq),
        jnp.sqrt(other_sq),
    )


def solution(mesh):
    placed = (
        P(("fsdp", "dp"), None),
        P(("fsdp", "dp"), None),
        P("fsdp"),
        P("fsdp"),
        P("fsdp", None),
        P("fsdp"),
        P("fsdp", None),
        P("fsdp"),
        P("fsdp"),
        P("fsdp"),
        P("fsdp", None),
        P("fsdp"),
        P("fsdp", None),
        P("fsdp"),
        P("fsdp"),
        P(("fsdp", "dp"), None),
    )
    return jax.shard_map(
        shards,
        mesh=mesh,
        in_specs=placed,
        out_specs=(
            P(("fsdp", "dp"), None),
            P(("fsdp", "dp"), None),
            P("fsdp"),
            P("fsdp"),
            P("fsdp", None),
            P("fsdp"),
            P("fsdp", None),
            P("fsdp"),
            P("fsdp"),
            P("fsdp"),
            P("fsdp", None),
            P("fsdp"),
            P("fsdp", None),
            P("fsdp"),
            P("fsdp"),
            P(),
            P(),
        ),
        check_vma=False,
    )
```

profile of v0, /device:TPU:0, one launch (start us, length us, event | category | flops | bytes accessed | tf_op | source)
XLA Modules:
  0.0 1132.7 jit_solution(17472799987714436141)
XLA Ops:
  19.5 40.6 %all-reduce.19 = (bf16[768]{0:T(1024)(128)(2,1)S(1)}, bf16[2304]{0:T(1024)(128)(2,1)S(1)}, bf16[768]{0:T(1024)(128)(2,1)S(1)}, bf16[768]{0:T(1024)(128)(2,1)S(1)...) all-reduce(bf16[768]{0:T(1024)(128)(2,1)S(1)} %dynamic-update-slice, ...), channel_id=1, replica_groups=mesh['fsdp'=8,'dp'=4] {'fsdp'}, use_global_device_ids=true, to_apply=%add.3 | all-reduce | flops 7680 | bytes 30720
  62.9 26.9 %all-gather = bf16[8,1,384]{2,1,0:T(2,128)(2,1)S(1)} all-gather(bf16[1,1,384]{2,1,0:T(2,128)(2,1)S(1)} %reshape.697), channel_id=1, replica_groups=mesh['fsdp'=8,'dp'=4] {'fsdp'}, dimensions={0}, use_global_device_ids=true | all-gather | bytes 6912 | tf_op jit(solution)/shard_map/all_gather | solution.py:183
  91.9 6.3 convolution_add_fusion
  109.7 10.8 fusion.87
  126.9 83.8 %while.48 = (s32[]{:T(128)}, bf16[12,1024,64]{1,2,0:T(8,128)(2,1)}, f32[12,1024]{1,0:T(8,128)S(1)}, s32[12]{0:T(128)S(1)}, bf16[1024,768]{1,0:T(8,128)(2,1)S(1)}...) while((s32[]{:T(128)}, bf16[12,1024,64]{1,2,0:T(8,128)(2,1)}, ...), condition=%wide.region_9.10_spmd.clone, body=%wide.region_6.9_spmd.clone.sunk | while | flops 283180032 | bytes 13558979 | solution.py:118
  210.8 3.9 fusion.98
  216.8 50.6 %fusion.44 = (bf16[1024,3072]{1,0:T(8,128)(2,1)}, f32[1024,3072]{1,0:T(8,128)}) fusion(f32[3072]{0:T(1024)S(1)} %bitcast.103, bf16[768,3072]{1,0:T(8,128)(2,1)} %all-gather.10.cloned.1.call-done, f32[1024,768]{0,1:T(8,128)} %copy-done.4, f32[768]{0:T(1024)S(1)} %convert_element_type.206, f32[768]{0:T(1024)S(1)} %convert_element_type.205, ...), kind=kOutput, calls=%fused_computation.50 | convolution fusion | flops 5043388416 | bytes 26765312 | tf_op jit(solution)/shard_map/dot_general | solution.py:15
  267.4 13.0 %all-gather.12.cloned.1.call-done = bf16[3072,768]{1,0:T(8,128)(2,1)} async-done(((bf16[384,768]{1,0:T(8,128)(2,1)}), bf16[3072,768]{1,0:T(8,128)(2,1)}) %all-gather.12.cloned.1.call-update) | async-done | bytes 4718608 | tf_op jit(solution)/shard_map/all_gather | solution.py:184
  280.4 11.9 %convert_reduce_fusion = (f32[3072]{0:T(1024)S(1)}, bf16[1024,3072]{1,0:T(8,128)(2,1)S(1)}) fusion(f32[1024,3072]{1,0:T(8,128)} %get-tuple-element.504, f32[3072]{0:T(1024)S(1)} %bitcast.104, bf16[1024,768]{1,0:T(8,128)(2,1)S(1)} %copy-done.15, bf16[3072,768]{1,0:T(8,128)(2,1)} %all-gather.12.cloned.1.call-done), kind=kOutput, calls=%fused_computation.57 | convolution fusion | flops 4872729600 | bytes 25190400 | tf_op jit(solution)/shard_map/dot_general | solution.py:25
  292.3 6.7 fusion.100
  312.6 4.5 convolution_convert_fusion
  317.1 230.8 %while.49 = (s32[]{:T(128)}, f32[12,1024,64]{1,2,0:T(8,128)}, f32[12,1024,64]{1,2,0:T(8,128)}, bf16[12,1024,64]{1,2,0:T(8,128)(2,1)}, s32[12]{0:T(128)S(1)}, /*i...) while((s32[]{:T(128)}, f32[12,1024,64]{1,2,0:T(8,128)}, ...), condition=%wide.region_16.17_spmd.clone, body=%wide.region_14.16_spmd.clone.sunk | while | flops 681704448 | bytes 50886960 | solution.py:143
  318.9 3.8 fusion.146
  324.6 3.9 multiply_reduce_fusion.22
  338.1 3.8 fusion.146
  343.8 3.9 multiply_reduce_fusion.22
  357.3 3.8 fusion.146
  363.0 3.9 multiply_reduce_fusion.22
  376.5 3.8 fusion.146
  382.2 3.9 multiply_reduce_fusion.22
  395.7 3.8 fusion.146
  401.4 3.9 multiply_reduce_fusion.22
  420.6 3.9 multiply_reduce_fusion.22
  439.8 3.9 multiply_reduce_fusion.22
  453.3 3.8 fusion.146
  459.0 3.9 multiply_reduce_fusion.22
  472.4 3.8 fusion.146
  478.2 3.9 multiply_reduce_fusion.22
  491.6 3.8 fusion.146
  497.3 3.9 multiply_reduce_fusion.22
  516.5 3.9 multiply_reduce_fusion.22
  529.9 3.8 fusion.146
  535.7 3.9 multiply_reduce_fusion.22
  547.9 12.2 %multiply_subtract_fusion = (f32[1024,12,32]{0,2,1:T(8,128)S(1)}, bf16[1024,12,32]{0,2,1:T(8,128)(2,1)S(1)}, bf16[1024,12,32]{0,2,1:T(8,128)(2,1)S(1)}, bf16[1024,12,32]{0,2,1:T(8,128)(2,1)S(1)}) fusion(f32[1024,12,64]{0,2,1:T(8,128)} %bitcast.87, f32[1024,12,64]{0,2,1:T(8,128)} %bitcast.97, f32[1024,12,64]{0,2,1:T(8,128)} %bitcast.86, ...), kind=kLoop, calls=%fused_computation.114 | loop fusion | flops 13762560 | bytes 16526336 | tf_op jit(solution)/shard_map/sub | solution.py:280
  560.2 6.4 multiply_reduce_fusion.7
  569.1 7.0 fusion.89
  576.2 10.6 fusion.93
  586.8 9.9 fusion.101
  599.3 10.1 add_convert_fusion
  612.1 8.6 fusion.99
  627.3 4.1 fusion.70
  636.2 35.3 %all-reduce.18 = (bf16[768]{0:T(1024)(128)(2,1)S(1)}, bf16[768]{0:T(1024)(128)(2,1)S(1)}, bf16[2304]{0:T(1024)(128)(2,1)S(1)}, bf16[768]{0:T(1024)(128)(2,1)S(1)...) all-reduce(f32[768]{0:T(1024)S(1)} %get-tuple-element.365, ...), channel_id=2, replica_groups=mesh['fsdp'=8,'dp'=4] {'fsdp'}, use_global_device_ids=true, to_apply=%region_20.21.clone | all-reduce | flops 10752 | bytes 64512
  672.2 6.1 all-reduce.20
  686.8 18.9 %reduce-scatter.5.cloned.1.call-done = f32[96,2304]{1,0:T(8,128)} async-done(((f32[768,2304]{1,0:T(8,128)}), f32[96,2304]{1,0:T(8,128)}) %reduce-scatter.5.cloned.1.call-update) | async-done | bytes 884752 | tf_op jit(solution)/shard_map/reduce_scatter | solution.py:314
  707.7 162.8 %reduce-scatter.9.cloned.1.call-done = f32[96,3072]{1,0:T(8,128)} async-done(((f32[768,3072]{1,0:T(8,128)}), f32[96,3072]{1,0:T(8,128)}) %reduce-scatter.9.cloned.1.call-update) | async-done | bytes 1179664 | tf_op jit(solution)/shard_map/reduce_scatter | solution.py:320
  872.6 162.7 %reduce-scatter.11.cloned.1.call-done = f32[384,768]{1,0:T(8,128)} async-done(((f32[3072,768]{1,0:T(8,128)}), f32[384,768]{1,0:T(8,128)}) %reduce-scatter.11.cloned.1.call-update) | async-done | bytes 1179664 | tf_op jit(solution)/shard_map/reduce_scatter | solution.py:322
  1042.2 42.1 %all-reduce.24.cloned.1.call-done = (bf16[96,2304]{1,0:T(8,128)(2,1)}, bf16[96,768]{1,0:T(8,128)(2,1)}, bf16[96,3072]{1,0:T(8,128)(2,1)}, bf16[384,768]{1,0:T(8,128)(2,1)}) async-done(((bf16[96,2304]{1,0:T(8,128)(2,1)}, bf16[96,768]{1,0:T(8,128)(2,1)}, bf16[96,3072]{1,0:T(8,128)(2,1)}, bf16[384,768]{1,0:T(8,128)(2,1)}), (bf16[96,2304]{1,0:T(8,128)(2,1)}, bf16[96,768]{1,0:T(8,128)(2,1)}, ...) | async-done | bytes 1769488 | tf_op jit(solution)/shard_map/psum | solution.py:329
  1100.3 22.0 %all-reduce.17 = (f32[]{:T(128)}, f32[]{:T(128)}) all-reduce(f32[]{:T(128)} %get-tuple-element.469, f32[]{:T(128)S(6)} %add.305), channel_id=1, replica_groups=mesh['fsdp'=8,'dp'=4] {'fsdp'}, use_global_device_ids=true, to_apply=%region_56.57 | all-reduce | flops 2 | bytes 16 | tf_op jit(solution)/shard_map/psum | solution.py:342
  (372 shorter events, 288.4 us)
Async XLA Ops:
  7.2 84.7 %all-gather.6.cloned.1.call-start = ((), (), s32[]{:S(2)}) async-start(), calls=%async_computation.4 | async-start | bytes 3981312 | tf_op jit(solution)/shard_map/all_gather | solution.py:176
  7.9 202.8 %all-gather.8.cloned.1.call-start = ((), (), s32[]{:S(2)}) async-start(), calls=%async_computation.5 | async-start | bytes 1327104 | tf_op jit(solution)/shard_map/all_gather | solution.py:178
  8.7 208.1 %all-gather.10.cloned.1.call-start = ((), (), s32[]{:S(2)}) async-start(), calls=%async_computation.6 | async-start | bytes 5308416 | tf_op jit(solution)/shard_map/all_gather | solution.py:182
  9.4 271.0 %all-gather.12.cloned.1.call-start = ((), (), s32[]{:S(2)}) async-start(), calls=%async_computation.7 | async-start | bytes 5308416 | tf_op jit(solution)/shard_map/all_gather | solution.py:184
  10.0 675.2 %reduce-scatter.7.cloned.1.call-start = ((), (), s32[]{:S(2)}) async-start(), calls=%async_computation.9 | async-start | bytes 2654208 | tf_op jit(solution)/shard_map/reduce_scatter | solution.py:316
  60.1 29.8 %copy-start.14 = (bf16[1024,768]{1,0:T(8,128)(2,1)S(1)}, bf16[1024,768]{1,0:T(8,128)(2,1)}, u32[]{:S(2)}) copy-start(bf16[1024,768]{1,0:T(8,128)(2,1)} %param.35) | copy-start | bytes 4718596
  61.9 148.8 %copy-start.1 = (bf16[1024,768]{0,1:T(8,128)(2,1)}, bf16[1024,768]{0,1:T(8,128)(2,1)S(1)}, u32[]{:S(2)}) copy-start(bf16[1024,768]{0,1:T(8,128)(2,1)S(1)} %copy.80) | copy-start | bytes 4718596
  61.9 29.9 %copy-start.32 = (f32[768]{0:T(1024)}, f32[768]{0:T(1024)S(1)}, u32[]{:S(2)}) copy-start(f32[768]{0:T(1024)S(1)} %convert_element_type.195) | copy-start | bytes 9220
  62.0 29.9 %copy-start.28 = (f32[768]{0:T(1024)}, f32[768]{0:T(1024)S(1)}, u32[]{:S(2)}) copy-start(f32[768]{0:T(1024)S(1)} %convert_element_type.194) | copy-start | bytes 9220
  62.2 36.0 %copy-start.22 = (f32[1024]{0:T(1024)}, f32[1024]{0:T(1024)S(1)}, u32[]{:S(2)}) copy-start(f32[1024]{0:T(1024)S(1)} %broadcast_multiply_fusion.5) | copy-start | bytes 12292
  62.7 35.5 %copy-start.30 = (f32[1024]{0:T(1024)}, f32[1024]{0:T(1024)S(1)}, u32[]{:S(2)}) copy-start(f32[1024]{0:T(1024)S(1)} %add_rsqrt_fusion.1) | copy-start | bytes 12292
  62.8 46.8 %copy-start.18 = (f32[12,32]{1,0:T(8,128)}, f32[12,32]{1,0:T(8,128)S(1)}, u32[]{:S(2)}) copy-start(f32[12,32]{1,0:T(8,128)S(1)} %slice.81) | copy-start | bytes 4612
  62.9 46.7 %copy-start.20 = (f32[12,32]{1,0:T(8,128)}, f32[12,32]{1,0:T(8,128)S(1)}, u32[]{:S(2)}) copy-start(f32[12,32]{1,0:T(8,128)S(1)} %slice.79) | copy-start | bytes 4612
  91.8 17.8 %copy-start.24 = (f32[1024]{0:T(1024)}, f32[1024]{0:T(1024)S(1)}, u32[]{:S(2)}) copy-start(f32[1024]{0:T(1024)S(1)} %get-tuple-element.490) | copy-start | bytes 12292
  91.8 17.8 %copy-start.26 = (f32[1024]{0:T(1024)}, f32[1024]{0:T(1024)S(1)}, u32[]{:S(2)}) copy-start(f32[1024]{0:T(1024)S(1)} %get-tuple-element.491) | copy-start | bytes 12292
  210.7 4.0 copy-start.10
  216.8 63.6 %copy-start.15 = (bf16[1024,768]{1,0:T(8,128)(2,1)S(1)}, bf16[1024,768]{1,0:T(8,128)(2,1)}, u32[]{:S(2)}) copy-start(bf16[1024,768]{1,0:T(8,128)(2,1)} %param.35) | copy-start | bytes 4718596
  280.4 11.9 %copy-start.37 = (bf16[768,3072]{1,0:T(8,128)(2,1)S(1)}, bf16[768,3072]{1,0:T(8,128)(2,1)}, u32[]{:S(2)}) copy-start(bf16[768,3072]{1,0:T(8,128)(2,1)} %all-gather.10.cloned.1.call-done) | copy-start | bytes 14155780
  292.3 6.8 copy-start.40
  299.0 3.7 copy-start.5
  302.8 3.1 copy-start.7
  302.8 3.3 copy-start.13
  306.1 3.5 copy-start.39
  309.5 3.1 copy-start.38
  312.4 393.3 %reduce-scatter.5.cloned.1.call-start = ((), (), s32[]{:S(2)}) async-start(), calls=%async_computation.8 | async-start | bytes 7962624 | tf_op jit(solution)/shard_map/reduce_scatter | solution.py:314
  317.1 230.8 %copy-start.3 = (f32[1024,768]{0,1:T(8,128)S(1)}, f32[1024,768]{0,1:T(8,128)}, u32[]{:S(2)}) copy-start(f32[1024,768]{0,1:T(8,128)} %copy.82) | copy-start | bytes 9437188
  317.1 230.8 %copy-start.19 = (f32[12,32]{1,0:T(8,128)S(1)}, f32[12,32]{1,0:T(8,128)}, u32[]{:S(2)}) copy-start(f32[12,32]{1,0:T(8,128)} %copy-done.18) | copy-start | bytes 4612
  317.1 230.8 %copy-start.21 = (f32[12,32]{1,0:T(8,128)S(1)}, f32[12,32]{1,0:T(8,128)}, u32[]{:S(2)}) copy-start(f32[12,32]{1,0:T(8,128)} %copy-done.20) | copy-start | bytes 4612
  317.1 230.8 %copy-start.25 = (f32[1024]{0:T(1024)S(1)}, f32[1024]{0:T(1024)}, u32[]{:S(2)}) copy-start(f32[1024]{0:T(1024)} %copy-done.24) | copy-start | bytes 12292
  317.1 230.8 %copy-start.27 = (f32[1024]{0:T(1024)S(1)}, f32[1024]{0:T(1024)}, u32[]{:S(2)}) copy-start(f32[1024]{0:T(1024)} %copy-done.26) | copy-start | bytes 12292
  324.6 3.9 copy-start
  343.8 4.0 copy-start
  363.0 3.9 copy-start
  382.2 3.9 copy-start
  401.4 3.9 copy-start
  420.6 3.9 copy-start
  439.8 3.9 copy-start
  459.0 3.9 copy-start
  478.2 3.9 copy-start
  497.3 3.9 copy-start
  516.5 3.9 copy-start
  535.7 3.9 copy-start
  547.9 12.2 %copy-start.8 = (f32[12,1024,64]{1,2,0:T(8,128)S(1)}, f32[12,1024,64]{1,2,0:T(8,128)}, u32[]{:S(2)}) copy-start(f32[12,1024,64]{1,2,0:T(8,128)} %get-tuple-element.173) | copy-start | bytes 9437188
  576.1 294.4 %reduce-scatter.9.cloned.1.call-start = ((), (), s32[]{:S(2)}) async-start(), calls=%async_computation.10 | async-start | bytes 10616832 | tf_op jit(solution)/shard_map/reduce_scatter | solution.py:320
  586.8 448.6 %reduce-scatter.11.cloned.1.call-start = ((), (), s32[]{:S(2)}) async-start(), calls=%async_computation.11 | async-start | bytes 10616832 | tf_op jit(solution)/shard_map/reduce_scatter | solution.py:322
  596.7 487.6 %all-reduce.24.cloned.1.call-start = ((), (), s32[]{:S(2)}) async-start(), calls=%async_computation.12 | async-start | bytes 3538944 | tf_op jit(solution)/shard_map/psum | solution.py:329
  624.2 3.1 copy-start.6
  1084.3 8.0 copy-start.17
  (13 other events, 27.6 us)
Sparse Core Ops, SparseCore 0:
  10.2 67.9 all-gather.5
  80.3 39.9 all-gather.7
  122.6 78.0 all-gather.9
  202.7 77.6 all-gather.11
  312.5 68.1 reduce-scatter.6
  576.2 129.4 reduce-scatter.4
  709.3 161.1 reduce-scatter.8
  874.1 161.1 reduce-scatter.10
  1039.1 45.1 all-reduce.23
where the time goes:
time: 1140 us; the launch traced here: 1130 us
  waiting for transfers between devices  402 us (35%)
  matrix products  366 us (32%)
  blocking collectives  131 us (11%)
  other arithmetic  101 us (9%)
  local copies, waits for them, and re-layouts  62 us (5%)
  loops' own time  40.6 us (4%)
  between operations  29.2 us (3%)
    reduce_scatter x1, waiting for transfers between devices, shards(): lax.psum_scatter(fc1_weight_grad, 'fsdp', scatter_dimension=0, tiled=True)  163 us
    reduce_scatter x1, waiting for transfers between devices, shards(): lax.psum_scatter(fc2_weight_grad, 'fsdp', scatter_dimension=0, tiled=True)  163 us
    dot_general x40, matrix products, matmul_right_t(): lax.dot_general(left, right, (((1,), (1,)), ((), ())), preferred_element_...  145 us
    dot_general x28, matrix products, matmul(): return jnp.dot(left, right, preferred_element_type=jnp.float32)  132 us
    dot_general x28, matrix products, matmul_left_t(): lax.dot_general(left, right, (((0,), (0,)), ((), ())), preferred_element_...  89.3 us
    unnamed x2, blocking collectives  75.9 us
    psum x1, waiting for transfers between devices, shards(): lax.psum(pieces[2].astype(jnp.bfloat16), 'dp').astype(jnp.float32)  42.1 us
    another operation x1, loops' own time, attend_bin_back(): d_query, d_key, d_value = lax.map(one_head, jnp.arange(H, dtype=jnp.int32))  32.2 us
  transfers between devices with their start and end apart: 9, of which 5 were waited for; matrix products, arithmetic and copies ran while one was open for 42% of the time, Pallas kernels for 0%

commit v1 on v0

--- a/solution.py
+++ b/solution.py
@@ -326,7 +326,7 @@
     pieces = (
         lax.psum(pieces[0].astype(jnp.bfloat16), "dp").astype(jnp.float32),
         lax.psum(pieces[1].astype(jnp.bfloat16), "dp").astype(jnp.float32),
-        lax.psum(pieces[2].astype(jnp.bfloat16), "dp").astype(jnp.float32),
+        jnp.sum(lax.all_gather(pieces[2].astype(jnp.bfloat16), "dp"), axis=0).astype(jnp.float32),
         lax.psum(pieces[3].astype(jnp.bfloat16), "dp").astype(jnp.float32),
         lax.psum(pieces[4].astype(jnp.bfloat16), "dp").astype(jnp.float32),
         lax.psum(pieces[5].astype(jnp.bfloat16), "dp").astype(jnp.float32),

time: 1140 us -> 1220 us (1.070)
  waiting for transfers between devices: 402 us -> 478 us
    reduce_scatter x1, waiting for transfers between devices: 18.9 us -> 71 us  [shards(): lax.psum_scatter(qkv_weight_grad, 'fsdp', scatter_dimension=0, tiled=True)]
    all_gather x0 -> x1, waiting for transfers between devices: none -> 17.5 us  [shards(): lax.all_gather(pieces[2].astype(jnp.bfloat16), 'dp')]
    unnamed x113 -> x107, local copies, waits for them, and re-layouts: 28 us -> 26.5 us
  transfers between devices with their start and end apart: 9 -> 10, of which waited for: 5 -> 7; matrix products, arithmetic and copies ran while one was open for 42% -> 22% of each run, Pallas kernels for 0% -> 0%
where the time goes in v1:
time: 1220 us; the launch traced here: 1210 us
  waiting for transfers between devices  478 us (39%)
  matrix products  367 us (30%)
  blocking collectives  131 us (11%)
  other arithmetic  104 us (9%)
  local copies, waits for them, and re-layouts  60.5 us (5%)
  loops' own time  40.5 us (3%)
  between operations  29.7 us (2%)
    reduce_scatter x1, waiting for transfers between devices, shards(): lax.psum_scatter(fc1_weight_grad, 'fsdp', scatter_dimension=0, tiled=True)  163 us
    reduce_scatter x1, waiting for transfers between devices, shards(): lax.psum_scatter(fc2_weight_grad, 'fsdp', scatter_dimension=0, tiled=True)  163 us
    dot_general x40, matrix products, matmul_right_t(): lax.dot_general(left, right, (((1,), (1,)), ((), ())), preferred_element_...  143 us
    dot_general x28, matrix products, matmul(): return jnp.dot(left, right, preferred_element_type=jnp.float32)  132 us
    dot_general x28, matrix products, matmul_left_t(): lax.dot_general(left, right, (((0,), (0,)), ((), ())), preferred_element_...  92 us
    unnamed x2, blocking collectives  76.8 us
    reduce_scatter x1, waiting for transfers between devices, shards(): lax.psum_scatter(qkv_weight_grad, 'fsdp', scatter_dimension=0, tiled=True)  71 us
    psum x1, waiting for transfers between devices, shards(): lax.psum(pieces[4].astype(jnp.bfloat16), 'dp').astype(jnp.float32)  38.5 us
  transfers between devices with their start and end apart: 10, of which 7 were waited for; matrix products, arithmetic and copies ran while one was open for 22% of the time, Pallas kernels for 0%

profile of v1, /device:TPU:0, one launch (start us, length us, event | category | flops | bytes accessed | tf_op | source)
XLA Modules:
  0.0 1210.5 jit_solution(13856684343744224451)
XLA Ops:
  19.5 40.6 %all-reduce.19 = (bf16[768]{0:T(1024)(128)(2,1)S(1)}, bf16[2304]{0:T(1024)(128)(2,1)S(1)}, bf16[768]{0:T(1024)(128)(2,1)S(1)}, bf16[768]{0:T(1024)(128)(2,1)S(1)...) all-reduce(bf16[768]{0:T(1024)(128)(2,1)S(1)} %dynamic-update-slice, ...), channel_id=1, replica_groups=mesh['fsdp'=8,'dp'=4] {'fsdp'}, use_global_device_ids=true, to_apply=%add.3 | all-reduce | flops 7680 | bytes 30720
  62.9 26.9 %all-gather.1 = bf16[8,1,384]{2,1,0:T(2,128)(2,1)S(1)} all-gather(bf16[1,1,384]{2,1,0:T(2,128)(2,1)S(1)} %reshape.698), channel_id=1, replica_groups=mesh['fsdp'=8,'dp'=4] {'fsdp'}, dimensions={0}, use_global_device_ids=true | all-gather | bytes 6912 | tf_op jit(solution)/shard_map/all_gather | solution.py:183
  91.9 6.3 convolution_add_fusion
  109.6 10.8 fusion.87
  127.0 83.8 %while.48 = (s32[]{:T(128)}, bf16[12,1024,64]{1,2,0:T(8,128)(2,1)}, f32[12,1024]{1,0:T(8,128)S(1)}, s32[12]{0:T(128)S(1)}, bf16[1024,768]{1,0:T(8,128)(2,1)S(1)}...) while((s32[]{:T(128)}, bf16[12,1024,64]{1,2,0:T(8,128)(2,1)}, ...), condition=%wide.region_9.10_spmd.clone, body=%wide.region_6.9_spmd.clone.sunk | while | flops 283180032 | bytes 13558979 | solution.py:118
  210.8 3.9 fusion.98
  216.9 50.6 %fusion.44 = (bf16[1024,3072]{1,0:T(8,128)(2,1)}, f32[1024,3072]{1,0:T(8,128)}) fusion(f32[3072]{0:T(1024)S(1)} %bitcast.105, bf16[768,3072]{1,0:T(8,128)(2,1)} %all-gather.12.cloned.1.call-done, f32[1024,768]{0,1:T(8,128)} %copy-done.4, f32[768]{0:T(1024)S(1)} %convert_element_type.208, f32[768]{0:T(1024)S(1)} %convert_element_type.207, ...), kind=kOutput, calls=%fused_computation.50 | convolution fusion | flops 5043388416 | bytes 26765312 | tf_op jit(solution)/shard_map/dot_general | solution.py:15
  267.5 12.9 %all-gather.14.cloned.1.call-done = bf16[3072,768]{1,0:T(8,128)(2,1)} async-done(((bf16[384,768]{1,0:T(8,128)(2,1)}), bf16[3072,768]{1,0:T(8,128)(2,1)}) %all-gather.14.cloned.1.call-update) | async-done | bytes 4718608 | tf_op jit(solution)/shard_map/all_gather | solution.py:184
  280.4 11.9 convert_reduce_fusion
  292.3 6.7 fusion.100
  310.5 230.6 %while.49 = (s32[]{:T(128)}, f32[12,1024,64]{1,2,0:T(8,128)}, f32[12,1024,64]{1,2,0:T(8,128)}, bf16[12,1024,64]{1,2,0:T(8,128)(2,1)}, s32[12]{0:T(128)S(1)}, /*i...) while((s32[]{:T(128)}, f32[12,1024,64]{1,2,0:T(8,128)}, ...), condition=%wide.region_16.17_spmd.clone, body=%wide.region_14.16_spmd.clone.sunk | while | flops 681704448 | bytes 50886960 | solution.py:143
  312.1 3.8 fusion.146
  317.9 3.9 multiply_reduce_fusion.22
  337.0 3.9 multiply_reduce_fusion.22
  350.5 3.8 fusion.146
  356.2 3.9 multiply_reduce_fusion.22
  369.7 3.8 fusion.146
  375.4 3.9 multiply_reduce_fusion.22
  394.6 3.9 multiply_reduce_fusion.22
  408.0 3.8 fusion.146
  413.8 3.9 multiply_reduce_fusion.22
  427.2 3.8 fusion.146
  433.0 3.9 multiply_reduce_fusion.22
  452.1 3.9 multiply_reduce_fusion.22
  465.6 3.8 fusion.146
  471.3 3.9 multiply_reduce_fusion.22
  490.5 3.9 multiply_reduce_fusion.22
  509.7 3.9 multiply_reduce_fusion.22
  523.1 3.8 fusion.146
  528.9 3.9 multiply_reduce_fusion.22
  541.1 12.2 %multiply_subtract_fusion = (f32[1024,12,32]{0,2,1:T(8,128)S(1)}, bf16[1024,12,32]{0,2,1:T(8,128)(2,1)S(1)}, bf16[1024,12,32]{0,2,1:T(8,128)(2,1)S(1)}, bf16[1024,12,32]{0,2,1:T(8,128)(2,1)S(1)}) fusion(f32[1024,12,64]{0,2,1:T(8,128)} %bitcast.88, f32[1024,12,64]{0,2,1:T(8,128)} %bitcast.98, f32[1024,12,64]{0,2,1:T(8,128)} %bitcast.87, ...), kind=kLoop, calls=%fused_computation.114 | loop fusion | flops 13762560 | bytes 16526336 | tf_op jit(solution)/shard_map/sub | solution.py:280
  553.4 6.4 multiply_reduce_fusion.7
  562.3 7.0 fusion.89
  569.4 5.2 fusion.82
  574.6 10.8 fusion.93
  585.5 9.9 fusion.101
  598.0 10.4 add_convert_fusion
  611.0 8.5 fusion.99
  626.0 71.0 %reduce-scatter.5.cloned.1.call-done = f32[96,2304]{1,0:T(8,128)} async-done(((f32[768,2304]{1,0:T(8,128)}), f32[96,2304]{1,0:T(8,128)}) %reduce-scatter.5.cloned.1.call-update) | async-done | bytes 884752 | tf_op jit(solution)/shard_map/reduce_scatter | solution.py:314
  699.0 5.0 fusion.70
  708.8 36.2 %all-reduce.18 = (bf16[768]{0:T(1024)(128)(2,1)S(1)}, bf16[768]{0:T(1024)(128)(2,1)S(1)}, bf16[2304]{0:T(1024)(128)(2,1)S(1)}, bf16[768]{0:T(1024)(128)(2,1)S(1)...) all-reduce(f32[768]{0:T(1024)S(1)} %get-tuple-element.365, ...), channel_id=3, replica_groups=mesh['fsdp'=8,'dp'=4] {'fsdp'}, use_global_device_ids=true, to_apply=%region_20.21.clone | all-reduce | flops 10752 | bytes 64512
  745.7 5.7 all-reduce.20
  760.7 9.0 reduce-scatter.7.cloned.1.call-done
  771.4 163.4 %reduce-scatter.9.cloned.1.call-done = f32[96,3072]{1,0:T(8,128)} async-done(((f32[768,3072]{1,0:T(8,128)}), f32[96,3072]{1,0:T(8,128)}) %reduce-scatter.9.cloned.1.call-update) | async-done | bytes 1179664 | tf_op jit(solution)/shard_map/reduce_scatter | solution.py:320
  936.9 162.7 %reduce-scatter.11.cloned.1.call-done = f32[384,768]{1,0:T(8,128)} async-done(((f32[3072,768]{1,0:T(8,128)}), f32[384,768]{1,0:T(8,128)}) %reduce-scatter.11.cloned.1.call-update) | async-done | bytes 1179664 | tf_op jit(solution)/shard_map/reduce_scatter | solution.py:322
  1104.1 17.5 %all-gather.16.cloned.1.call-done = bf16[384,2304]{1,0:T(8,128)(2,1)} async-done(((bf16[96,2304]{1,0:T(8,128)(2,1)}), bf16[384,2304]{1,0:T(8,128)(2,1)}) %all-gather.16.cloned.1.call-update) | async-done | bytes 1769488 | tf_op jit(solution)/shard_map/all_gather | solution.py:329
  1126.3 38.5 %all-reduce.24.cloned.1.call-done = (bf16[96,768]{1,0:T(8,128)(2,1)}, bf16[96,3072]{1,0:T(8,128)(2,1)}, bf16[384,768]{1,0:T(8,128)(2,1)}) async-done(((bf16[96,768]{1,0:T(8,128)(2,1)}, bf16[96,3072]{1,0:T(8,128)(2,1)}, bf16[384,768]{1,0:T(8,128)(2,1)}), (bf16[96,768]{1,0:T(8,128)(2,1)}, bf16[96,3072]{1,0:T(8,128)(2,1)}, bf16[384,768]{1,0:T(8,128)(2,1)})) %all-reduce.24.cloned.1.call-update) | async-done | bytes 1327120 | tf_op jit(solution)/shard_map/psum | solution.py:331
  1177.8 22.0 %all-reduce.17 = (f32[]{:T(128)}, f32[]{:T(128)}) all-reduce(f32[]{:T(128)} %get-tuple-element.468, f32[]{:T(128)S(6)} %add.303), channel_id=1, replica_groups=mesh['fsdp'=8,'dp'=4] {'fsdp'}, use_global_device_ids=true, to_apply=%region_56.57 | all-reduce | flops 2 | bytes 16 | tf_op jit(solution)/shard_map/psum | solution.py:342
  (370 shorter events, 295.6 us)
Async XLA Ops:
  7.2 84.7 %all-gather.8.cloned.1.call-start = ((), (), s32[]{:S(2)}) async-start(), calls=%async_computation.4 | async-start | bytes 3981312 | tf_op jit(solution)/shard_map/all_gather | solution.py:176
  7.9 202.9 %all-gather.10.cloned.1.call-start = ((), (), s32[]{:S(2)}) async-start(), calls=%async_computation.5 | async-start | bytes 1327104 | tf_op jit(solution)/shard_map/all_gather | solution.py:178
  8.7 208.2 %all-gather.12.cloned.1.call-start = ((), (), s32[]{:S(2)}) async-start(), calls=%async_computation.6 | async-start | bytes 5308416 | tf_op jit(solution)/shard_map/all_gather | solution.py:182
  9.4 270.9 %all-gather.14.cloned.1.call-start = ((), (), s32[]{:S(2)}) async-start(), calls=%async_computation.7 | async-start | bytes 5308416 | tf_op jit(solution)/shard_map/all_gather | solution.py:184
  10.0 687.0 %reduce-scatter.5.cloned.1.call-start = ((), (), s32[]{:S(2)}) async-start(), calls=%async_computation.8 | async-start | bytes 7962624 | tf_op jit(solution)/shard_map/reduce_scatter | solution.py:314
  60.0 2.8 copy-start.33
  60.0 2.9 copy-start.34
  60.1 29.8 %copy-start.13 = (bf16[1024,768]{1,0:T(8,128)(2,1)S(1)}, bf16[1024,768]{1,0:T(8,128)(2,1)}, u32[]{:S(2)}) copy-start(bf16[1024,768]{1,0:T(8,128)(2,1)} %param.35) | copy-start | bytes 4718596
  61.9 148.9 %copy-start.1 = (bf16[1024,768]{0,1:T(8,128)(2,1)}, bf16[1024,768]{0,1:T(8,128)(2,1)S(1)}, u32[]{:S(2)}) copy-start(bf16[1024,768]{0,1:T(8,128)(2,1)S(1)} %copy.80) | copy-start | bytes 4718596
  61.9 29.9 %copy-start.30 = (f32[768]{0:T(1024)}, f32[768]{0:T(1024)S(1)}, u32[]{:S(2)}) copy-start(f32[768]{0:T(1024)S(1)} %convert_element_type.197) | copy-start | bytes 9220
  62.0 29.9 %copy-start.26 = (f32[768]{0:T(1024)}, f32[768]{0:T(1024)S(1)}, u32[]{:S(2)}) copy-start(f32[768]{0:T(1024)S(1)} %convert_element_type.196) | copy-start | bytes 9220
  62.2 36.0 %copy-start.20 = (f32[1024]{0:T(1024)}, f32[1024]{0:T(1024)S(1)}, u32[]{:S(2)}) copy-start(f32[1024]{0:T(1024)S(1)} %broadcast_multiply_fusion.5) | copy-start | bytes 12292
  62.7 35.5 %copy-start.28 = (f32[1024]{0:T(1024)}, f32[1024]{0:T(1024)S(1)}, u32[]{:S(2)}) copy-start(f32[1024]{0:T(1024)S(1)} %add_rsqrt_fusion.1) | copy-start | bytes 12292
  62.8 46.8 %copy-start.16 = (f32[12,32]{1,0:T(8,128)}, f32[12,32]{1,0:T(8,128)S(1)}, u32[]{:S(2)}) copy-start(f32[12,32]{1,0:T(8,128)S(1)} %slice.81) | copy-start | bytes 4612
  62.9 46.7 %copy-start.18 = (f32[12,32]{1,0:T(8,128)}, f32[12,32]{1,0:T(8,128)S(1)}, u32[]{:S(2)}) copy-start(f32[12,32]{1,0:T(8,128)S(1)} %slice.79) | copy-start | bytes 4612
  91.8 17.8 %copy-start.22 = (f32[1024]{0:T(1024)}, f32[1024]{0:T(1024)S(1)}, u32[]{:S(2)}) copy-start(f32[1024]{0:T(1024)S(1)} %get-tuple-element.489) | copy-start | bytes 12292
  91.8 17.8 %copy-start.24 = (f32[1024]{0:T(1024)}, f32[1024]{0:T(1024)S(1)}, u32[]{:S(2)}) copy-start(f32[1024]{0:T(1024)S(1)} %get-tuple-element.490) | copy-start | bytes 12292
  210.8 4.0 copy-start.9
  216.8 63.5 %copy-start.14 = (bf16[1024,768]{1,0:T(8,128)(2,1)S(1)}, bf16[1024,768]{1,0:T(8,128)(2,1)}, u32[]{:S(2)}) copy-start(bf16[1024,768]{1,0:T(8,128)(2,1)} %param.35) | copy-start | bytes 4718596
  280.4 11.9 copy-start.35
  292.2 6.8 copy-start.37
  299.0 3.7 copy-start.5
  302.7 3.1 copy-start.6
  302.7 3.3 copy-start.12
  310.5 230.6 %copy-start.3 = (f32[1024,768]{0,1:T(8,128)S(1)}, f32[1024,768]{0,1:T(8,128)}, u32[]{:S(2)}) copy-start(f32[1024,768]{0,1:T(8,128)} %copy.82) | copy-start | bytes 9437188
  310.5 230.6 %copy-start.17 = (f32[12,32]{1,0:T(8,128)S(1)}, f32[12,32]{1,0:T(8,128)}, u32[]{:S(2)}) copy-start(f32[12,32]{1,0:T(8,128)} %copy-done.16) | copy-start | bytes 4612
  310.5 230.6 %copy-start.19 = (f32[12,32]{1,0:T(8,128)S(1)}, f32[12,32]{1,0:T(8,128)}, u32[]{:S(2)}) copy-start(f32[12,32]{1,0:T(8,128)} %copy-done.18) | copy-start | bytes 4612
  310.5 230.6 %copy-start.23 = (f32[1024]{0:T(1024)S(1)}, f32[1024]{0:T(1024)}, u32[]{:S(2)}) copy-start(f32[1024]{0:T(1024)} %copy-done.22) | copy-start | bytes 12292
  310.5 230.6 %copy-start.25 = (f32[1024]{0:T(1024)S(1)}, f32[1024]{0:T(1024)}, u32[]{:S(2)}) copy-start(f32[1024]{0:T(1024)} %copy-done.24) | copy-start | bytes 12292
  317.9 3.9 copy-start
  337.0 3.9 copy-start
  356.2 3.9 copy-start
  375.4 3.9 copy-start
  394.6 3.9 copy-start
  413.7 3.9 copy-start
  432.9 3.9 copy-start
  452.1 3.9 copy-start
  471.3 3.9 copy-start
  490.5 3.9 copy-start
  509.7 3.9 copy-start
  528.9 3.9 copy-start
  541.1 12.2 %copy-start.7 = (f32[12,1024,64]{1,2,0:T(8,128)S(1)}, f32[12,1024,64]{1,2,0:T(8,128)}, u32[]{:S(2)}) copy-start(f32[12,1024,64]{1,2,0:T(8,128)} %get-tuple-element.173) | copy-start | bytes 9437188
  569.3 200.5 %reduce-scatter.7.cloned.1.call-start = ((), (), s32[]{:S(2)}) async-start(), calls=%async_computation.9 | async-start | bytes 2654208 | tf_op jit(solution)/shard_map/reduce_scatter | solution.py:316
  574.6 360.2 %reduce-scatter.9.cloned.1.call-start = ((), (), s32[]{:S(2)}) async-start(), calls=%async_computation.10 | async-start | bytes 10616832 | tf_op jit(solution)/shard_map/reduce_scatter | solution.py:320
  585.4 514.2 %reduce-scatter.11.cloned.1.call-start = ((), (), s32[]{:S(2)}) async-start(), calls=%async_computation.11 | async-start | bytes 10616832 | tf_op jit(solution)/shard_map/reduce_scatter | solution.py:322
  595.4 526.2 %all-gather.16.cloned.1.call-start = ((), (), s32[]{:S(2)}) async-start(), calls=%async_computation.12 | async-start | bytes 2211840 | tf_op jit(solution)/shard_map/all_gather | solution.py:329
  699.0 465.8 %all-reduce.24.cloned.1.call-start = ((), (), s32[]{:S(2)}) async-start(), calls=%async_computation.13 | async-start | bytes 2654208 | tf_op jit(solution)/shard_map/psum | solution.py:331
  704.0 2.9 copy-start.11
  (11 other events, 21.9 us)
Sparse Core Ops, SparseCore 0:
  10.2 67.9 all-gather.7
  80.3 40.1 all-gather.9
  122.8 77.7 all-gather.11
  202.6 77.6 all-gather.13
  569.4 127.4 reduce-scatter.4
  700.3 69.4 reduce-scatter.6
  773.4 161.3 reduce-scatter.8
  938.4 161.1 reduce-scatter.10
  1101.7 19.8 all-gather.15
  1125.1 39.5 all-reduce.23
